TPU v7x, 512 devices: a whole 4x8x8 slice. The times are simulated.
512 devices in a mesh: fsdp: 8 (over z_hi, core), seq: 64 (over z_lo, x, y).
Axes of the slice: x: 4, y: 8, z: 8 (z_hi: 4, z_lo: 2; z = z_hi * 2 + z_lo), core: 2. Of those that a mesh axis runs over, the one named last changes fastest.
Arguments:
- hidden: bfloat16 [8192, 8192], P('seq', 'fsdp'), may hold values from -6 to 6
- queries: bfloat16 [8192, 8192], P('seq', 'fsdp'), may hold values from -160 to 160
- kv_weight: bfloat16 [8192, 2048], P('fsdp'), may hold values from -0.09375 to 0.09375
- kv_bias: float32 [2048], replicated, may hold values from -5 to 5
- parents: int32 [64], replicated, may hold values from 0 to 62, as said below
- slot_block: int32 [64], replicated, may hold values from 0 to 63, each once
Outputs:
- attended: bfloat16 [8192, 8192], P('seq', 'fsdp')
Inputs may be any that keep to these rules, and one draw needn't show every extreme that they name: parents[0] = 0; every other block's parent has a lower number; blocks below 32 form one chain from block 0.
All inputs are finite; a program needn't handle non-finite values.
Results may differ from a plain program's by a relative error of at most 0.018.
Values may be sent and summed in bfloat16 or wider, within the bound.
No kernel may reach another device: no remote copies, remote signals or barrier semaphores. Data moves between devices by JAX's collectives and lax.ppermute only.
A program may use at most 64 MiB of HBM per device.

v0:
```python
import math
import jax
import jax.numpy as jnp
from jax import lax
from jax.sharding import PartitionSpec as P

HD = 128
BLOCK = 128


def ancestry_table(parents, slot_block):
    block_count = parents.shape[0]
    block_ids = jnp.arange(block_count, dtype=jnp.int32)
    linked = (parents[:, None] == block_ids[None, :]).astype(jnp.float32)
    ancestry = jnp.maximum(jnp.eye(block_count, dtype=jnp.float32), linked)
    for sweep in range(block_count.bit_length()):
        ancestry = jnp.minimum(jnp.dot(ancestry, ancestry, precision=lax.Precision.HIGHEST), 1.0)
    placement = (slot_block[:, None] == block_ids[None, :]).astype(jnp.float32)
    first_pass = jnp.dot(placement, ancestry, precision=lax.Precision.HIGHEST)
    return jnp.dot(first_pass, placement.T, precision=lax.Precision.HIGHEST)


def keep_state(state_now):
    return state_now


def shards(hidden, queries, kv_weight, kv_bias, parents, slot_block):
    tok_rows = hidden.shape[0]
    per_device = tok_rows // BLOCK
    head_count = queries.shape[1] // HD
    score_scale = 1.0 / math.sqrt(HD)
    fsdp_index = lax.axis_index("fsdp")
    partial_sums = jnp.dot(hidden, kv_weight, preferred_element_type=jnp.float32)
    head_bias = lax.dynamic_slice_in_dim(kv_bias, fsdp_index * 2 * HD, 2 * HD, 0)
    summed = lax.psum(partial_sums, "fsdp")
    head_cols = lax.dynamic_slice_in_dim(summed, fsdp_index * 2 * HD, 2 * HD, 1)
    both_parts = (head_cols + head_bias).astype(jnp.bfloat16)
    key_rows = both_parts[:, :HD]
    value_rows = both_parts[:, HD:]
    visible = ancestry_table(parents, slot_block)
    first_slot = lax.axis_index("seq") * per_device
    own_visible = lax.dynamic_slice_in_dim(visible, first_slot, per_device, 0)
    row_slot = first_slot + jnp.arange(tok_rows, dtype=jnp.int32) // BLOCK
    row_offset = jnp.arange(tok_rows, dtype=jnp.int32) % BLOCK
    query_heads = queries.reshape(tok_rows, head_count, HD)
    initial = (
        jnp.full((tok_rows, head_count), -1e30, jnp.float32),
        jnp.zeros((tok_rows, head_count), jnp.float32),
        jnp.zeros((tok_rows, head_count, HD), jnp.float32),
    )
    key_piece = lax.all_gather(key_rows, "seq", axis=0, tiled=True)
    value_piece = lax.all_gather(value_rows, "seq", axis=0, tiled=True)
    piece_blocks = key_piece.shape[0] // BLOCK
    group = math.gcd(piece_blocks, 8)
    tile = group * BLOCK
    tile_count = piece_blocks // group
    key_offset = jnp.arange(tile, dtype=jnp.int32) % BLOCK
    key_inner = jnp.arange(tile, dtype=jnp.int32) // BLOCK

    def one_tile(tile_index, state_now):
        key_slot_first = tile_index * group
        tile_visible = lax.dynamic_slice_in_dim(own_visible, key_slot_first, group, 1)

        def attend(state_in):
            running_max, running_sum, numerator = state_in
            key_tile = lax.dynamic_slice_in_dim(key_piece, tile_index * tile, tile, 0)
            value_tile = lax.dynamic_slice_in_dim(value_piece, tile_index * tile, tile, 0)
            scores = (
                jnp.einsum("qhd,kd->qhk", query_heads, key_tile, preferred_element_type=jnp.float32)
                * score_scale
            )
            spread = jnp.repeat(jnp.repeat(tile_visible, BLOCK, axis=0), BLOCK, axis=1) > 0.5
            key_slot = key_slot_first + key_inner
            allowed = spread & (
                (row_slot[:, None] != key_slot[None, :])
                | (key_offset[None, :] <= row_offset[:, None])
            )
            masked = jnp.where(allowed[:, None, :], scores, -1e30)
            new_max = jnp.maximum(running_max, jnp.max(masked, axis=-1))
            expo = jnp.where(allowed[:, None, :], jnp.exp(masked - new_max[..., None]), 0.0)
            factor = jnp.exp(running_max - new_max)
            new_sum = running_sum * factor + jnp.sum(expo, axis=-1)
            update = jnp.einsum(
                "qhk,kd->qhd",
                expo.astype(jnp.bfloat16),
                value_tile,
                preferred_element_type=jnp.float32,
            )
            new_numerator = numerator * factor[..., None] + update
            return (new_max, new_sum, new_numerator)

        return lax.cond(jnp.max(tile_visible) > 0.5, attend, keep_state, state_now)

    final_max, final_sum, final_numerator = lax.fori_loop(0, tile_count, one_tile, initial)
    attended = final_numerator / final_sum[..., None]
    return attended.reshape(tok_rows, head_count * HD).astype(jnp.bfloat16)


def solution(mesh):
    return jax.shard_map(
        shards,
        mesh=mesh,
        in_specs=(P("seq", "fsdp"), P("seq", "fsdp"), P("fsdp", None), P(), P(), P()),
        out_specs=P("seq", "fsdp"),
        check_vma=False,
    )
```

profile of v0, /device:TPU:8, one launch (start us, length us, event | category | flops | bytes accessed | tf_op | source)
XLA Modules:
  0.0 772.2 jit_solution(17489612144787789115)
XLA Ops:
  7.5 3.9 fusion.43
  12.2 87.0 %all-reduce.2.cloned.1.call-done = f32[128,2048]{1,0:T(8,128)} async-done(((f32[128,2048]{1,0:T(8,128)}), f32[128,2048]{1,0:T(8,128)}) %all-reduce.2.cloned.1.call-update) | async-done | bytes 1048592 | tf_op jit(solution)/shard_map/psum | solution.py:35
  103.7 297.8 %all-gather.3.cloned.1.call-done = bf16[8192,128]{1,0:T(8,128)(2,1)} async-done(((bf16[128,128]{1,0:T(8,128)(2,1)}), bf16[8192,128]{1,0:T(8,128)(2,1)}) %all-gather.3.cloned.1.call-update) | async-done | bytes 2097168 | tf_op jit(solution)/shard_map/all_gather | solution.py:51
  401.5 301.9 %all-gather.5.cloned.1.call-done = bf16[8192,128]{1,0:T(8,128)(2,1)} async-done(((bf16[128,128]{1,0:T(8,128)(2,1)}), bf16[8192,128]{1,0:T(8,128)(2,1)}) %all-gather.5.cloned.1.call-update) | async-done | bytes 2097168 | tf_op jit(solution)/shard_map/all_gather | solution.py:52
  703.4 61.3 %while.18 = (s32[]{:T(128)}, f32[128,8]{0,1:T(8,128)S(1)}, f32[128,8]{0,1:T(8,128)S(1)}, f32[128,8,128]{2,0,1:T(8,128)S(1)}, f32[1,64]{1,0:T(1,128)S(1)}, /*inde...) while((s32[]{:T(128)}, f32[128,8]{0,1:T(8,128)S(1)}, ...), condition=%wide.region_7.8_spmd.clone, body=%wide.region_1.7_spmd.clone.sunk | while | flops 551307008 | bytes 15081951 | solution.py:94
  704.9 6.2 conditional.3
  705.9 1.7 fusion.8
  707.6 1.0 fusion.10
  708.7 2.4 fusion.14
  712.6 6.2 conditional.3
  713.6 1.7 fusion.8
  715.3 1.0 fusion.10
  716.3 2.4 fusion.14
  720.2 6.2 conditional.3
  721.2 1.7 fusion.8
  723.0 1.0 fusion.10
  724.0 2.4 fusion.14
  727.9 6.2 conditional.3
  728.9 1.7 fusion.8
  731.7 2.4 fusion.14
  735.6 6.2 conditional.3
  736.6 1.7 fusion.8
  739.3 2.4 fusion.14
  743.2 6.2 conditional.3
  744.2 1.7 fusion.8
  747.0 2.4 fusion.14
  750.9 6.2 conditional.3
  751.9 1.7 fusion.8
  754.7 2.4 fusion.14
  758.6 6.2 conditional.3
  759.6 1.7 fusion.8
  762.3 2.4 fusion.14
  (174 shorter events, 25.9 us)
Async XLA Ops:
  6.5 1.0 copy-start
  6.5 95.0 %copy-start.1 = (bf16[128,1024]{1,0:T(8,128)(2,1)S(1)}, bf16[128,1024]{1,0:T(8,128)(2,1)}, u32[]{:S(2)}) copy-start(bf16[128,1024]{1,0:T(8,128)(2,1)} %param.11) | copy-start | bytes 786436
  6.5 95.4 %copy-start.3 = (s32[64]{0:T(128)S(1)}, s32[64]{0:T(128)}, u32[]{:S(2)}) copy-start(s32[64]{0:T(128)} %param.14) | copy-start | bytes 772
  6.5 96.6 %copy-start.2 = (s32[64]{0:T(128)S(1)}, s32[64]{0:T(128)}, u32[]{:S(2)}) copy-start(s32[64]{0:T(128)} %param.15) | copy-start | bytes 772
  6.5 92.7 %all-reduce.2.cloned.1.call-start = ((), (), s32[]{:S(2)}) async-start(), calls=%async_computation | async-start | bytes 2097152 | tf_op jit(solution)/shard_map/psum | solution.py:35
  11.4 390.1 %all-gather.3.cloned.1.call-start = ((), (), s32[]{:S(2)}) async-start(), calls=%async_computation.1 | async-start | bytes 2129920 | tf_op jit(solution)/shard_map/all_gather | solution.py:51
  100.8 602.6 %all-gather.5.cloned.1.call-start = ((), (), s32[]{:S(2)}) async-start(), calls=%async_computation.2 | async-start | bytes 2129920 | tf_op jit(solution)/shard_map/all_gather | solution.py:52
Sparse Core Ops, SparseCore 0:
  11.5 87.6 all-reduce.1
  101.3 300.1 all-gather.2
  403.6 299.7 all-gather.4
where the time goes:
time: 773 us; the launch traced here: 772 us
  waiting for transfers between devices  687 us (89%)
  matrix products  38.3 us (5%)
  other arithmetic  23 us (3%)
  between operations  13.3 us (2%)
    all_gather x1, waiting for transfers between devices, shards(): value_piece = lax.all_gather(value_rows, 'seq', axis=0, tiled=True)  302 us
    all_gather x1, waiting for transfers between devices, shards(): key_piece = lax.all_gather(key_rows, 'seq', axis=0, tiled=True)  298 us
    psum x1, waiting for transfers between devices, shards(): summed = lax.psum(partial_sums, 'fsdp')  87 us
    dot_general x8, matrix products, attend(): jnp.einsum('qhk,kd->qhd', expo.astype(jnp.bfloat16), value_tile, preferre...  19.1 us
  transfers between devices with their start and end apart: 3, of which 3 were waited for; matrix products, arithmetic and copies ran while one was open for 0% of the time, Pallas kernels for 0%

commit v1 on v0

--- a/solution.py
+++ b/solution.py
@@ -49,7 +49,9 @@
         jnp.zeros((tok_rows, head_count, HD), jnp.float32),
     )
     key_piece = lax.all_gather(key_rows, "seq", axis=0, tiled=True)
-    value_piece = lax.all_gather(value_rows, "seq", axis=0, tiled=True)
+    value_piece = jnp.concatenate(
+        lax.all_to_all(jnp.stack([value_rows] * lax.axis_size("seq")), "seq", 0, 0), axis=0
+    )
     piece_blocks = key_piece.shape[0] // BLOCK
     group = math.gcd(piece_blocks, 8)
     tile = group * BLOCK

time: 773 us -> 478 us (0.62)
  waiting for transfers between devices: 687 us -> 390 us
  starting transfers between devices: 0.12 us -> 10.6 us
    all_gather x1 -> x0, waiting for transfers between devices: 302 us -> none  [shards(): value_piece = lax.all_gather(value_rows, 'seq', axis=0, tiled=True)]
    all_to_all x0 -> x1, waiting for transfers between devices: none -> 51.2 us  [shards(): lax.all_to_all(jnp.stack([value_rows] * lax.axis_size('seq')), 'seq', 0, 0)]
    all_gather x1, waiting for transfers between devices: 298 us -> 251 us  [shards(): key_piece = lax.all_gather(key_rows, 'seq', axis=0, tiled=True)]
    all_to_all x0 -> x1, starting transfers between devices: none -> 10.5 us  [shards(): lax.all_to_all(jnp.stack([value_rows] * lax.axis_size('seq')), 'seq', 0, 0)]
  transfers between devices with their start and end apart: 3 -> 3, of which waited for: 3 -> 3; matrix products, arithmetic and copies ran while one was open for 0% -> 1% of each run, Pallas kernels for 0% -> 0%
where the time goes in v1:
time: 478 us
  waiting for transfers between devices  390 us (82%)
  matrix products  30.6 us (6%)
  other arithmetic  22.3 us (5%)
  between operations  13.6 us (3%)
  starting transfers between devices  10.6 us (2%)
  loops' own time  5.63 us (1%)
  local copies, waits for them, and re-layouts  5.29 us (1%)
    all_gather x1, waiting for transfers between devices, shards(): key_piece = lax.all_gather(key_rows, 'seq', axis=0, tiled=True)  251 us
    psum x1, waiting for transfers between devices, shards(): summed = lax.psum(partial_sums, 'fsdp')  87 us
    all_to_all x1, waiting for transfers between devices, shards(): lax.all_to_all(jnp.stack([value_rows] * lax.axis_size('seq')), 'seq', 0, 0)  51.2 us
    dot_general x8, matrix products, attend(): jnp.einsum('qhd,kd->qhk', query_heads, key_tile, preferred_element_type=j...  13.7 us
    dot_general x8, matrix products, attend(): jnp.einsum('qhk,kd->qhd', expo.astype(jnp.bfloat16), value_tile, preferre...  11.4 us
    all_to_all x1, starting transfers between devices, shards(): lax.all_to_all(jnp.stack([value_rows] * lax.axis_size('seq')), 'seq', 0, 0)  10.5 us
  transfers between devices with their start and end apart: 3, of which 3 were waited for; matrix products, arithmetic and copies ran while one was open for 1% of the time, Pallas kernels for 0%

profile of v1, /device:TPU:8, one launch (start us, length us, event | category | flops | bytes accessed | tf_op | source)
XLA Modules:
  0.0 477.5 jit_solution(13947221437388648741)
XLA Ops:
  7.5 3.9 fusion.43
  12.2 87.0 %all-reduce.2.cloned.1.call-done = f32[128,2048]{1,0:T(8,128)} async-done(((f32[128,2048]{1,0:T(8,128)}), f32[128,2048]{1,0:T(8,128)}) %all-reduce.2.cloned.1.call-update) | async-done | bytes 1048592 | tf_op jit(solution)/shard_map/psum | solution.py:35
  100.8 1.8 stack.2
  102.6 10.5 %all-to-all-start = ((bf16[64,128,128]{2,1,0:T(8,128)(2,1)}), bf16[64,128,128]{2,1,0:T(8,128)(2,1)S(1)}, u32[]{:S(2)}, u32[]{:S(2)}) async-start(bf16[64,128,128]{2,1,0:T(8,128)(2,1)} %stack.2), calls=%async_computation | async-start | bytes 4194304 | tf_op jit(solution)/shard_map/all_to_all | solution.py:53
  116.0 51.2 %all-to-all-done = bf16[64,128,128]{2,1,0:T(8,128)(2,1)S(1)} async-done(((bf16[64,128,128]{2,1,0:T(8,128)(2,1)}), bf16[64,128,128]{2,1,0:T(8,128)(2,1)S(1)}, u32[]{:S(2)}, u32[]{:S(2)}) %all-to-all-start) | async-done | bytes 2097184 | tf_op jit(solution)/shard_map/all_to_all | solution.py:53
  167.3 250.7 %all-gather.2.cloned.1.call-done = bf16[8192,128]{1,0:T(8,128)(2,1)} async-done(((bf16[128,128]{1,0:T(8,128)(2,1)}), bf16[8192,128]{1,0:T(8,128)(2,1)}) %all-gather.2.cloned.1.call-update) | async-done | bytes 2097168 | tf_op jit(solution)/shard_map/all_gather | solution.py:51
  418.0 51.8 %while.18 = (s32[]{:T(128)}, f32[128,8]{0,1:T(8,128)S(1)}, f32[128,8]{0,1:T(8,128)S(1)}, f32[128,8,128]{2,0,1:T(8,128)S(1)}, f32[1,64]{1,0:T(1,128)S(1)}, /*inde...) while((s32[]{:T(128)}, f32[128,8]{0,1:T(8,128)S(1)}, ...), condition=%wide.region_7.8_spmd.clone, body=%wide.region_1.7_spmd.clone.sunk | while | flops 551307008 | bytes 15081951 | solution.py:96
  419.2 5.2 %conditional.3 = ((f32[128,8]{0,1:T(8,128)S(1)}, f32[128,8]{0,1:T(8,128)S(1)}, f32[128,8,128]{2,0,1:T(8,128)S(1)})) conditional(s32[]{:T(128)} %convert_element_type.51, (f32[128,8]{0,1:T(8,128)S(1)}, f32[128,8]{0,1:T(8,128)S(1)}, f32[128,8,128]{2,0,1:T(8,128)S(1)}) %tuple.59, (f32[1,8]{1,0:T(1,128)S(1)}, s32[]{:T(128)}, s32[]{:T(128)}, ...), branch_computations={%region_3.3_spmd, %region_4.6_spmd.clone} | conditional | flops 551302400 | bytes 15061798 | solution.py:94
  420.2 1.7 fusion.8
  422.0 1.0 fusion.10
  423.0 1.4 fusion.14
  425.7 5.2 %conditional.3 = ((f32[128,8]{0,1:T(8,128)S(1)}, f32[128,8]{0,1:T(8,128)S(1)}, f32[128,8,128]{2,0,1:T(8,128)S(1)})) conditional(s32[]{:T(128)} %convert_element_type.51, (f32[128,8]{0,1:T(8,128)S(1)}, f32[128,8]{0,1:T(8,128)S(1)}, f32[128,8,128]{2,0,1:T(8,128)S(1)}) %tuple.59, (f32[1,8]{1,0:T(1,128)S(1)}, s32[]{:T(128)}, s32[]{:T(128)}, ...), branch_computations={%region_3.3_spmd, %region_4.6_spmd.clone} | conditional | flops 551302400 | bytes 15061798 | solution.py:94
  426.7 1.7 fusion.8
  429.5 1.4 fusion.14
  432.2 5.2 %conditional.3 = ((f32[128,8]{0,1:T(8,128)S(1)}, f32[128,8]{0,1:T(8,128)S(1)}, f32[128,8,128]{2,0,1:T(8,128)S(1)})) conditional(s32[]{:T(128)} %convert_element_type.51, (f32[128,8]{0,1:T(8,128)S(1)}, f32[128,8]{0,1:T(8,128)S(1)}, f32[128,8,128]{2,0,1:T(8,128)S(1)}) %tuple.59, (f32[1,8]{1,0:T(1,128)S(1)}, s32[]{:T(128)}, s32[]{:T(128)}, ...), branch_computations={%region_3.3_spmd, %region_4.6_spmd.clone} | conditional | flops 551302400 | bytes 15061798 | solution.py:94
  433.2 1.7 fusion.8
  435.9 1.4 fusion.14
  438.7 5.2 %conditional.3 = ((f32[128,8]{0,1:T(8,128)S(1)}, f32[128,8]{0,1:T(8,128)S(1)}, f32[128,8,128]{2,0,1:T(8,128)S(1)})) conditional(s32[]{:T(128)} %convert_element_type.51, (f32[128,8]{0,1:T(8,128)S(1)}, f32[128,8]{0,1:T(8,128)S(1)}, f32[128,8,128]{2,0,1:T(8,128)S(1)}) %tuple.59, (f32[1,8]{1,0:T(1,128)S(1)}, s32[]{:T(128)}, s32[]{:T(128)}, ...), branch_computations={%region_3.3_spmd, %region_4.6_spmd.clone} | conditional | flops 551302400 | bytes 15061798 | solution.py:94
  439.7 1.7 fusion.8
  442.4 1.4 fusion.14
  445.1 5.2 %conditional.3 = ((f32[128,8]{0,1:T(8,128)S(1)}, f32[128,8]{0,1:T(8,128)S(1)}, f32[128,8,128]{2,0,1:T(8,128)S(1)})) conditional(s32[]{:T(128)} %convert_element_type.51, (f32[128,8]{0,1:T(8,128)S(1)}, f32[128,8]{0,1:T(8,128)S(1)}, f32[128,8,128]{2,0,1:T(8,128)S(1)}) %tuple.59, (f32[1,8]{1,0:T(1,128)S(1)}, s32[]{:T(128)}, s32[]{:T(128)}, ...), branch_computations={%region_3.3_spmd, %region_4.6_spmd.clone} | conditional | flops 551302400 | bytes 15061798 | solution.py:94
  446.1 1.7 fusion.8
  448.9 1.4 fusion.14
  451.6 5.2 %conditional.3 = ((f32[128,8]{0,1:T(8,128)S(1)}, f32[128,8]{0,1:T(8,128)S(1)}, f32[128,8,128]{2,0,1:T(8,128)S(1)})) conditional(s32[]{:T(128)} %convert_element_type.51, (f32[128,8]{0,1:T(8,128)S(1)}, f32[128,8]{0,1:T(8,128)S(1)}, f32[128,8,128]{2,0,1:T(8,128)S(1)}) %tuple.59, (f32[1,8]{1,0:T(1,128)S(1)}, s32[]{:T(128)}, s32[]{:T(128)}, ...), branch_computations={%region_3.3_spmd, %region_4.6_spmd.clone} | conditional | flops 551302400 | bytes 15061798 | solution.py:94
  452.6 1.7 fusion.8
  455.4 1.4 fusion.14
  458.1 5.2 %conditional.3 = ((f32[128,8]{0,1:T(8,128)S(1)}, f32[128,8]{0,1:T(8,128)S(1)}, f32[128,8,128]{2,0,1:T(8,128)S(1)})) conditional(s32[]{:T(128)} %convert_element_type.51, (f32[128,8]{0,1:T(8,128)S(1)}, f32[128,8]{0,1:T(8,128)S(1)}, f32[128,8,128]{2,0,1:T(8,128)S(1)}) %tuple.59, (f32[1,8]{1,0:T(1,128)S(1)}, s32[]{:T(128)}, s32[]{:T(128)}, ...), branch_computations={%region_3.3_spmd, %region_4.6_spmd.clone} | conditional | flops 551302400 | bytes 15061798 | solution.py:94
  459.1 1.7 fusion.8
  461.9 1.4 fusion.14
  464.6 5.2 %conditional.3 = ((f32[128,8]{0,1:T(8,128)S(1)}, f32[128,8]{0,1:T(8,128)S(1)}, f32[128,8,128]{2,0,1:T(8,128)S(1)})) conditional(s32[]{:T(128)} %convert_element_type.51, (f32[128,8]{0,1:T(8,128)S(1)}, f32[128,8]{0,1:T(8,128)S(1)}, f32[128,8,128]{2,0,1:T(8,128)S(1)}) %tuple.59, (f32[1,8]{1,0:T(1,128)S(1)}, s32[]{:T(128)}, s32[]{:T(128)}, ...), branch_computations={%region_3.3_spmd, %region_4.6_spmd.clone} | conditional | flops 551302400 | bytes 15061798 | solution.py:94
  465.6 1.7 fusion.8
  468.3 1.4 fusion.14
  (174 shorter events, 27.1 us)
Async XLA Ops:
  6.5 1.0 copy-start
  6.5 92.7 %all-reduce.2.cloned.1.call-start = ((), (), s32[]{:S(2)}) async-start(), calls=%async_computation.1 | async-start | bytes 2097152 | tf_op jit(solution)/shard_map/psum | solution.py:35
  11.4 102.5 %copy-start.1 = (bf16[128,1024]{1,0:T(8,128)(2,1)S(1)}, bf16[128,1024]{1,0:T(8,128)(2,1)}, u32[]{:S(2)}) copy-start(bf16[128,1024]{1,0:T(8,128)(2,1)} %param.11) | copy-start | bytes 786436
  11.4 102.9 %copy-start.3 = (s32[64]{0:T(128)S(1)}, s32[64]{0:T(128)}, u32[]{:S(2)}) copy-start(s32[64]{0:T(128)} %param.14) | copy-start | bytes 772
  12.2 103.3 %copy-start.2 = (s32[64]{0:T(128)S(1)}, s32[64]{0:T(128)}, u32[]{:S(2)}) copy-start(s32[64]{0:T(128)} %param.15) | copy-start | bytes 772
  102.6 64.7 %all-to-all-start = ((bf16[64,128,128]{2,1,0:T(8,128)(2,1)}), bf16[64,128,128]{2,1,0:T(8,128)(2,1)S(1)}, u32[]{:S(2)}, u32[]{:S(2)}) async-start(bf16[64,128,128]{2,1,0:T(8,128)(2,1)} %stack.2), calls=%async_computation | async-start | bytes 4194304 | tf_op jit(solution)/shard_map/all_to_all | solution.py:53
  113.2 304.8 %all-gather.2.cloned.1.call-start = ((), (), s32[]{:S(2)}) async-start(), calls=%async_computation.2 | async-start | bytes 2129920 | tf_op jit(solution)/shard_map/all_gather | solution.py:51
Sparse Core Ops, SparseCore 0:
  11.5 87.6 all-reduce.1
  116.1 301.8 all-gather.1
